TPU v7x, 128 devices: a whole 4x4x4 slice. The times are simulated.
128 devices in a mesh: row: 8 (over z_hi, x), col: 16 (over z_lo, y, core).
Axes of the slice: x: 4, y: 4, z: 4 (z_hi: 2, z_lo: 2; z = z_hi * 2 + z_lo), core: 2. Of those that a mesh axis runs over, the one named last changes fastest.
Arguments:
- tokens: bfloat16 [1024, 8192], P(('row', 'col')), may hold values from -6 to 6
- gain: float32 [8192], replicated, may hold values from 0.5 to 1.5
- grad_out: bfloat16 [1024, 8192], P(('row', 'col')), may hold values from -4 to 4
- pre_gate: bfloat16 [1024, 28672], P('col', 'row'), may hold values from -6 to 6
- pre_up: bfloat16 [1024, 28672], P('col', 'row'), may hold values from -6 to 6
- gate_weight: bfloat16 [8192, 28672], P('col', 'row'), may hold values from -0.0625 to 0.0625
- up_weight: bfloat16 [8192, 28672], P('col', 'row'), may hold values from -0.0625 to 0.0625
- down_weight: bfloat16 [28672, 8192], P('row', 'col'), may hold values from -0.03125 to 0.03125
Outputs:
- grad_tokens: bfloat16 [1024, 8192], P(('row', 'col'))
- grad_gain: float32 [8192], replicated
- grad_gate: bfloat16 [8192, 28672], P('col', 'row')
- grad_up: bfloat16 [8192, 28672], P('col', 'row')
- grad_down: bfloat16 [28672, 8192], P('row', 'col')
All inputs are finite; a program needn't handle non-finite values.
Results may differ from a plain program's by a relative error of at most 0.0057.
Values may be sent and summed in bfloat16 or wider, within the bound.
No kernel may reach another device: no remote copies, remote signals or barrier semaphores. Data moves between devices by JAX's collectives and lax.ppermute only.
A program may use at most 192 MiB of HBM per device.

v0:
```python
import jax
import jax.numpy as jnp
from jax import lax
from jax.sharding import PartitionSpec as P

epsilon = 1e-05


def swiglu_grads(hidden_grad, pre_gate, pre_up):
    gate_wide = pre_gate.astype(jnp.float32)
    up_wide = pre_up.astype(jnp.float32)
    sigmoid = jax.nn.sigmoid(gate_wide)
    silu = gate_wide * sigmoid
    hidden = (silu * up_wide).astype(jnp.bfloat16)
    up_grad = (hidden_grad * silu).astype(jnp.bfloat16)
    gate_grad = (hidden_grad * up_wide * sigmoid * (1.0 + gate_wide * (1.0 - sigmoid))).astype(
        jnp.bfloat16
    )
    return (hidden, gate_grad, up_grad)


def row_gather(x):
    rows = lax.axis_size("row")
    copies = jnp.broadcast_to(x[None], (rows,) + x.shape)
    got = lax.all_to_all(copies, "row", split_axis=0, concat_axis=0, tiled=True)
    return got.reshape((rows * x.shape[0],) + x.shape[1:])


def local(tokens, gain, grad_out, pre_gate, pre_up, gate_weight, up_weight, down_weight):
    cols = lax.axis_size("col")
    rows = lax.axis_size("row")
    tokens_wide = tokens.astype(jnp.float32)
    inverse_rms = lax.rsqrt(jnp.mean(tokens_wide * tokens_wide, axis=1, keepdims=True) + epsilon)
    normed = tokens_wide * inverse_rms
    tile = gate_weight.shape[0]
    gain_tile = lax.dynamic_slice_in_dim(gain, lax.axis_index("col") * tile, tile)
    mine_rows = tokens.shape[0]
    lanes = 128
    grid_grad = lax.all_to_all(grad_out, "col", split_axis=1, concat_axis=0, tiled=True)
    packed = jnp.concatenate(
        [
            tokens_wide.reshape(mine_rows, cols, tile),
            jnp.broadcast_to(inverse_rms[:, :, None], (mine_rows, cols, lanes)),
        ],
        axis=2,
    )
    grid = lax.all_to_all(packed, "col", split_axis=1, concat_axis=0, tiled=True)
    grid = grid.reshape(cols * mine_rows, tile + lanes)
    grid_tokens = grid[:, :tile].astype(jnp.bfloat16)
    grid_scale = grid[:, tile : tile + 1].reshape(1, cols * mine_rows)
    all_grad = row_gather(grid_grad)
    hidden_block = swiglu_grads(jnp.zeros(pre_gate.shape, jnp.float32), pre_gate, pre_up)[0]
    split = hidden_block.shape[1] // 448 * 128
    hidden_piece = lax.all_gather(hidden_block[:, :split], "col", axis=0, tiled=True)
    partial_grad = jnp.einsum(
        "td,fd->tf", all_grad, down_weight, preferred_element_type=jnp.float32
    )
    hidden_piece, partial_grad = lax.optimization_barrier((hidden_piece, partial_grad))
    block_grad = lax.psum_scatter(partial_grad, "col", scatter_dimension=0, tiled=True)
    down_total = jnp.einsum("tf,td->fd", hidden_piece, all_grad, preferred_element_type=jnp.float32)
    down_total, block_grad = lax.optimization_barrier((down_total, block_grad))
    _, gate_block, up_block = swiglu_grads(block_grad, pre_gate, pre_up)
    all_tokens = row_gather(grid_tokens).astype(jnp.float32)
    all_scale = row_gather(grid_scale).reshape(-1, 1)
    all_normed = all_tokens * all_scale
    all_input = (all_normed * gain_tile).astype(jnp.bfloat16)
    gate_piece = lax.all_gather(gate_block, "col", axis=0, tiled=True)
    up_piece = lax.all_gather(up_block, "col", axis=0, tiled=True)
    gate_total = jnp.einsum("td,tf->df", all_input, gate_piece, preferred_element_type=jnp.float32)
    gate_total, up_piece = lax.optimization_barrier((gate_total, up_piece))
    late_block, up_piece = lax.optimization_barrier((hidden_block[:, split:], up_piece))
    late_piece = lax.all_gather(late_block, "col", axis=0, tiled=True)
    new_rows = jnp.einsum("tf,df->td", gate_piece, gate_weight, preferred_element_type=jnp.float32)
    new_rows = new_rows + jnp.einsum(
        "tf,df->td", up_piece, up_weight, preferred_element_type=jnp.float32
    )
    gain_part = jnp.sum(new_rows * all_normed, axis=0)
    tokens_all = new_rows.shape[0]
    blocks = new_rows.astype(jnp.bfloat16).reshape(rows, tokens_all // rows, tile)
    gain_high = gain_part.astype(jnp.bfloat16)
    gain_low = (gain_part - gain_high.astype(jnp.float32)).astype(jnp.bfloat16)
    extra = jnp.zeros((rows, 8, tile), jnp.bfloat16)
    extra = extra.at[:, 0, :].set(gain_high).at[:, 1, :].set(gain_low)
    sent = jnp.concatenate([blocks, extra], axis=1)
    got = lax.all_to_all(sent, "row", split_axis=0, concat_axis=0, tiled=True)
    summed = jnp.sum(got.astype(jnp.float32), axis=0)
    grid_back = summed[: tokens_all // rows]
    gain_tile_grad = summed[tokens_all // rows] + summed[tokens_all // rows + 1]
    per_col = grid_back.reshape(cols, -1, tile)
    mine = per_col.shape[1]
    sent2 = jnp.concatenate(
        [per_col, jnp.broadcast_to(gain_tile_grad[None, None, :], (cols, 1, tile))], axis=1
    )
    got2 = lax.all_to_all(sent2, "col", split_axis=0, concat_axis=0, tiled=True)
    normed_grad = got2[:, :mine, :].transpose(1, 0, 2).reshape(mine, cols * tile)
    grad_gain = got2[:, mine, :].reshape(cols * tile)
    up_total = jnp.einsum("td,tf->df", all_input, up_piece, preferred_element_type=jnp.float32)
    down_late = jnp.einsum("tf,td->fd", late_piece, all_grad, preferred_element_type=jnp.float32)
    scaled_grad = normed_grad * gain
    inner = jnp.mean(scaled_grad * normed, axis=1, keepdims=True)
    grad_tokens = (
        grad_out.astype(jnp.float32) + inverse_rms * (scaled_grad - normed * inner)
    ).astype(jnp.bfloat16)
    return (
        grad_tokens,
        grad_gain,
        gate_total.astype(jnp.bfloat16),
        up_total.astype(jnp.bfloat16),
        jnp.concatenate([down_total, down_late], axis=0).astype(jnp.bfloat16),
    )


def solution(mesh):
    in_specs = (
        P(("row", "col"), None),
        P(),
        P(("row", "col"), None),
        P("col", "row"),
        P("col", "row"),
        P("col", "row"),
        P("col", "row"),
        P("row", "col"),
    )
    out_specs = (P(("row", "col"), None), P(), P("col", "row"), P("col", "row"), P("row", "col"))
    return jax.shard_map(local, mesh=mesh, in_specs=in_specs, out_specs=out_specs, check_vma=False)
```

profile of v0, /device:TPU:1, one launch (start us, length us, event | category | flops | bytes accessed | tf_op | source)
XLA Modules:
  0.0 330.3 jit_solution(11313620677822065228)
XLA Ops:
  7.2 0.0 all-gather.5.cloned.1.call-start
  7.2 1.4 fusion.4
  8.6 0.7 slice.76
  9.3 0.0 reduce-scatter.2.cloned.1.call-start
  9.4 13.4 %all_to_all.56 = bf16[8,16,512]{2,0,1:T(8,128)(2,1)S(1)} all-to-all(bf16[8,16,512]{2,0,1:T(8,128)(2,1)} %bitcast.49), channel_id=1, replica_groups=mesh['row'=8,'col'=16] {'col'}, dimensions={1} | all-to-all | bytes 262144 | tf_op jit(solution)/shard_map/all_to_all | solution.py:39
  22.8 0.1 broadcast_in_dim.15
  22.9 23.5 %all_to_all.57 = bf16[8,128,512]{2,1,0:T(8,128)(2,1)S(1)} all-to-all(bf16[8,128,512]{2,1,0:T(8,128)(2,1)S(1)} %broadcast_in_dim.15), channel_id=1, replica_groups=mesh['row'=8,'col'=16] {'row'}, dimensions={0} | all-to-all | bytes 2097152 | tf_op jit(solution)/shard_map/all_to_all | solution.py:25
  46.4 1.0 copy-done.4
  47.4 9.4 %fusion.13 = f32[1024,3584]{1,0:T(8,128)} fusion(bf16[1024,512]{1,0:T(8,128)(2,1)S(1)} %bitcast.42, bf16[3584,512]{1,0:T(8,128)(2,1)} %param.19), kind=kOutput, calls=%fused_computation.38 | convolution fusion | flops 3758096384 | bytes 19398656 | tf_op jit(solution)/shard_map/td,fd->tf/dot_general | solution.py:55
  56.8 0.0 reduce-scatter.2.cloned.1.call-update
  56.8 0.0 all-gather.7.cloned.1.call-start
  56.9 3.2 fusion.14
  60.1 84.9 %reduce-scatter.2.cloned.1.call-done = f32[64,3584]{1,0:T(8,128)} async-done(((f32[1024,3584]{1,0:T(8,128)}), f32[64,3584]{1,0:T(8,128)}) %reduce-scatter.2.cloned.1.call-update) | async-done | bytes 917520 | tf_op jit(solution)/shard_map/reduce_scatter | solution.py:59
  145.0 2.5 multiply_convert_fusion
  147.5 0.0 all-gather.9.cloned.1.call-start
  147.6 0.5 all-gather.9.cloned.1.call-update
  148.2 0.2 multiply_reduce_fusion.1
  148.3 0.1 broadcast_in_dim.16
  148.5 14.1 %all_to_all.58 = f32[8,16,640]{2,0,1:T(8,128)S(1)} all-to-all(f32[8,16,640]{2,0,1:T(8,128)S(1)} %pad_maximum_fusion.3), channel_id=1, replica_groups=mesh['row'=8,'col'=16] {'col'}, dimensions={1} | all-to-all | bytes 655360 | tf_op jit(solution)/shard_map/all_to_all | solution.py:47
  162.6 0.1 slice_reduce_fusion
  162.7 0.6 broadcast_in_dim.19
  163.3 6.3 %all-to-all-start.4 = ((f32[8,1,128]{2,1,0:T(1,128)}), f32[8,1,128]{2,1,0:T(1,128)S(1)}, u32[]{:S(2)}, u32[]{:S(2)}) async-start(f32[8,1,128]{2,1,0:T(1,128)} %broadcast_in_dim.19), calls=%async_computation.5 | async-start | bytes 8192 | tf_op jit(solution)/shard_map/all_to_all | solution.py:25
  169.6 6.4 %all-to-all-done.4 = f32[8,1,128]{2,1,0:T(1,128)S(1)} async-done(((f32[8,1,128]{2,1,0:T(1,128)}), f32[8,1,128]{2,1,0:T(1,128)S(1)}, u32[]{:S(2)}, u32[]{:S(2)}) %all-to-all-start.4) | async-done | bytes 4128 | tf_op jit(solution)/shard_map/all_to_all | solution.py:25
  176.1 1.1 broadcast_in_dim.17
  177.1 3.6 %all-to-all-start.3 = ((bf16[8,128,512]{2,1,0:T(8,128)(2,1)}), bf16[8,128,512]{2,1,0:T(8,128)(2,1)S(1)}, u32[]{:S(2)}, u32[]{:S(2)}) async-start(bf16[8,128,512]{2,1,0:T(8,128)(2,1)} %broadcast_in_dim.17), calls=%async_computation.4 | async-start | bytes 2097152 | tf_op jit(solution)/shard_map/all_to_all | solution.py:25
  180.7 0.2 all-gather.11.cloned.1.call-start
  180.9 0.7 slice.77
  181.7 0.1 dynamic_slice.3
  181.8 16.7 %all-to-all-done.3 = bf16[8,128,512]{2,1,0:T(8,128)(2,1)S(1)} async-done(((bf16[8,128,512]{2,1,0:T(8,128)(2,1)}), bf16[8,128,512]{2,1,0:T(8,128)(2,1)S(1)}, u32[]{:S(2)}, u32[]{:S(2)}) %all-to-all-start.3) | async-done | bytes 1048608 | tf_op jit(solution)/shard_map/all_to_all | solution.py:25
  198.5 1.3 fusion.2
  199.7 10.2 %all-gather.7.cloned.1.call-done = bf16[1024,3584]{1,0:T(8,128)(2,1)} async-done(((bf16[64,3584]{1,0:T(8,128)(2,1)}), bf16[1024,3584]{1,0:T(8,128)(2,1)}) %all-gather.7.cloned.1.call-update) | async-done | bytes 7340048 | tf_op jit(solution)/shard_map/all_gather | solution.py:67
  209.9 9.3 %fusion.16 = bf16[512,3584]{1,0:T(8,128)(2,1)} fusion(bf16[1024,512]{1,0:T(8,128)(2,1)} %fusion.2, bf16[1024,3584]{1,0:T(8,128)(2,1)} %all-gather.7.cloned.1.call-done), kind=kOutput, calls=%fused_computation.41 | convolution fusion | flops 3758096384 | bytes 12058624 | tf_op jit(solution)/shard_map/td,tf->df/dot_general | solution.py:69
  219.1 39.1 %all-gather.9.cloned.1.call-done = bf16[1024,3584]{1,0:T(8,128)(2,1)} async-done(((bf16[64,3584]{1,0:T(8,128)(2,1)}), bf16[1024,3584]{1,0:T(8,128)(2,1)}) %all-gather.9.cloned.1.call-update) | async-done | bytes 7340048 | tf_op jit(solution)/shard_map/all_gather | solution.py:68
  258.2 7.5 %fusion.15 = f32[1024,512]{1,0:T(8,128)S(1)} fusion(bf16[1024,3584]{1,0:T(8,128)(2,1)} %all-gather.7.cloned.1.call-done, bf16[512,3584]{1,0:T(8,128)(2,1)} %param.17), kind=kOutput, calls=%fused_computation.40 | convolution fusion | flops 3758096384 | bytes 13107200 | tf_op jit(solution)/shard_map/tf,df->td/dot_general | solution.py:73
  265.8 5.1 %fusion.12 = (bf16[1024,512]{1,0:T(8,128)(2,1)}, f32[512]{0:T(512)S(1)}) fusion(f32[1024]{0:T(1024)S(1)} %bitcast.52, bf16[8,128,512]{2,1,0:T(8,128)(2,1)S(1)} %all-to-all-done.3, f32[1024,512]{1,0:T(8,128)S(1)} %fusion.15, bf16[1024,3584]{1,0:T(8,128)(2,1)S(1)} %copy-done.7, bf16[512,3584]{1,0:T(8,128)(2,1)S(1)} %copy-done.8), kind=kOutput, calls=%fused_computation.37 | convolution fusion | flops 3761241600 | bytes 15210496 | tf_op jit(solution)/shard_map/tf,df->td/dot_general | solution.py:74
  270.9 0.1 scatter.9
  271.0 1.4 pad_maximum_fusion.1
  272.4 25.1 %all_to_all.59 = bf16[8,136,512]{2,1,0:T(8,128)(2,1)S(1)} all-to-all(bf16[8,136,512]{2,1,0:T(8,128)(2,1)S(1)} %pad_maximum_fusion.1), channel_id=1, replica_groups=mesh['row'=8,'col'=16] {'row'}, dimensions={0} | all-to-all | bytes 2228224 | tf_op jit(solution)/shard_map/all_to_all | solution.py:85
  297.5 0.2 convert_reduce_fusion
  297.8 0.9 pad_maximum_fusion.2
  298.6 5.4 %all-to-all-start.6 = ((f32[16,9,512]{2,1,0:T(8,128)}), f32[16,9,512]{2,1,0:T(8,128)S(1)}, u32[]{:S(2)}, u32[]{:S(2)}) async-start(f32[16,9,512]{2,1,0:T(8,128)} %pad_maximum_fusion.2), calls=%async_computation.7 | async-start | bytes 1048576 | tf_op jit(solution)/shard_map/all_to_all | solution.py:94
  304.0 8.7 %convolution_convert_fusion = bf16[512,3584]{1,0:T(8,128)(2,1)} fusion(bf16[1024,512]{1,0:T(8,128)(2,1)S(1)} %copy-done.3, bf16[1024,3584]{1,0:T(8,128)(2,1)} %all-gather.9.cloned.1.call-done), kind=kOutput, calls=%fused_computation | convolution fusion | flops 3759931392 | bytes 12058624 | tf_op jit(solution)/shard_map/td,tf->df/dot_general | solution.py:97
  312.7 1.6 all-to-all-done.6
  314.3 0.6 slice.84
  314.9 0.3 multiply_reduce_fusion
  315.2 0.8 add_convert_fusion
  316.0 5.7 %convolution_convert_fusion.1 = bf16[2560,512]{1,0:T(8,128)(2,1)S(1)} fusion(bf16[1024,2560]{1,0:T(8,128)(2,1)} %all-gather.11.cloned.1.call-done, bf16[1024,512]{1,0:T(8,128)(2,1)} %bitcast.44), kind=kOutput, calls=%fused_computation.1 | convolution fusion | flops 2685665280 | bytes 8912896 | tf_op jit(solution)/shard_map/tf,td->fd/dot_general | solution.py:98
  321.7 2.1 pad_maximum_fusion
  (35 shorter events, 0.3 us)
Async XLA Ops:
  7.2 49.6 %all-gather.5.cloned.1.call-start = ((), (), s32[]{:S(2)}) async-start(), calls=%async_computation.8 | async-start | bytes 2228224 | tf_op jit(solution)/shard_map/all_gather | solution.py:54
  9.3 135.6 %reduce-scatter.2.cloned.1.call-start = ((), (), s32[]{:S(2)}) async-start(), calls=%async_computation.9 | async-start | bytes 15597568 | tf_op jit(solution)/shard_map/reduce_scatter | solution.py:59
  46.4 1.0 copy-start.4
  56.8 88.2 %copy-start.1 = (bf16[64,3584]{1,0:T(8,128)(2,1)S(1)}, bf16[64,3584]{1,0:T(8,128)(2,1)}, u32[]{:S(2)}) copy-start(bf16[64,3584]{1,0:T(8,128)(2,1)} %param.16) | copy-start | bytes 1376260
  56.8 88.1 %copy-start.2 = (bf16[64,3584]{1,0:T(8,128)(2,1)S(1)}, bf16[64,3584]{1,0:T(8,128)(2,1)}, u32[]{:S(2)}) copy-start(bf16[64,3584]{1,0:T(8,128)(2,1)} %param.15) | copy-start | bytes 1376260
  56.8 153.1 %all-gather.7.cloned.1.call-start = ((), (), s32[]{:S(2)}) async-start(), calls=%async_computation.10 | async-start | bytes 7798784 | tf_op jit(solution)/shard_map/all_gather | solution.py:67
  60.1 88.0 %copy-start = (bf16[8,8192]{1,0:T(8,128)(2,1)S(1)}, bf16[8,8192]{1,0:T(8,128)(2,1)}, u32[]{:S(2)}) copy-start(bf16[8,8192]{1,0:T(8,128)(2,1)} %param.12) | copy-start | bytes 393220
  147.5 34.2 %copy-start.6 = (f32[8192]{0:T(1024)S(1)}, f32[8192]{0:T(1024)}, u32[]{:S(2)}) copy-start(f32[8192]{0:T(1024)} %param.13) | copy-start | bytes 98308
  147.5 110.7 %all-gather.9.cloned.1.call-start = ((), (), s32[]{:S(2)}) async-start(), calls=%async_computation.11 | async-start | bytes 7798784 | tf_op jit(solution)/shard_map/all_gather | solution.py:68
  163.3 12.8 %all-to-all-start.4 = ((f32[8,1,128]{2,1,0:T(1,128)}), f32[8,1,128]{2,1,0:T(1,128)S(1)}, u32[]{:S(2)}, u32[]{:S(2)}) async-start(f32[8,1,128]{2,1,0:T(1,128)} %broadcast_in_dim.19), calls=%async_computation.5 | async-start | bytes 8192 | tf_op jit(solution)/shard_map/all_to_all | solution.py:25
  177.1 21.3 %all-to-all-start.3 = ((bf16[8,128,512]{2,1,0:T(8,128)(2,1)}), bf16[8,128,512]{2,1,0:T(8,128)(2,1)S(1)}, u32[]{:S(2)}, u32[]{:S(2)}) async-start(bf16[8,128,512]{2,1,0:T(8,128)(2,1)} %broadcast_in_dim.17), calls=%async_computation.4 | async-start | bytes 2097152 | tf_op jit(solution)/shard_map/all_to_all | solution.py:25
  180.7 135.2 %all-gather.11.cloned.1.call-start = ((), (), s32[]{:S(2)}) async-start(), calls=%async_computation.12 | async-start | bytes 5570560 | tf_op jit(solution)/shard_map/all_gather | solution.py:72
  258.2 7.5 %copy-start.7 = (bf16[1024,3584]{1,0:T(8,128)(2,1)S(1)}, bf16[1024,3584]{1,0:T(8,128)(2,1)}, u32[]{:S(2)}) copy-start(bf16[1024,3584]{1,0:T(8,128)(2,1)} %all-gather.9.cloned.1.call-done) | copy-start | bytes 22020100
  258.2 7.5 %copy-start.8 = (bf16[512,3584]{1,0:T(8,128)(2,1)S(1)}, bf16[512,3584]{1,0:T(8,128)(2,1)}, u32[]{:S(2)}) copy-start(bf16[512,3584]{1,0:T(8,128)(2,1)} %param.18) | copy-start | bytes 11010052
  271.0 33.0 %copy-start.3 = (bf16[1024,512]{1,0:T(8,128)(2,1)S(1)}, bf16[1024,512]{1,0:T(8,128)(2,1)}, u32[]{:S(2)}) copy-start(bf16[1024,512]{1,0:T(8,128)(2,1)} %fusion.2) | copy-start | bytes 3145732
  298.6 15.6 %all-to-all-start.6 = ((f32[16,9,512]{2,1,0:T(8,128)}), f32[16,9,512]{2,1,0:T(8,128)S(1)}, u32[]{:S(2)}, u32[]{:S(2)}) async-start(f32[16,9,512]{2,1,0:T(8,128)} %pad_maximum_fusion.2), calls=%async_computation.7 | async-start | bytes 1048576 | tf_op jit(solution)/shard_map/all_to_all | solution.py:94
  304.0 11.2 %copy-start.5 = (bf16[8,8192]{1,0:T(8,128)(2,1)S(1)}, bf16[8,8192]{1,0:T(8,128)(2,1)}, u32[]{:S(2)}) copy-start(bf16[8,8192]{1,0:T(8,128)(2,1)} %param.14) | copy-start | bytes 393220
Sparse Core Ops, SparseCore 0:
  10.2 45.7 all-gather.4
  58.4 86.4 reduce-scatter.1
  147.7 62.1 all-gather.6
  211.4 46.7 all-gather.8
  259.8 56.1 all-gather.10
where the time goes:
time: 331 us; the launch traced here: 330 us
  waiting for transfers between devices  159 us (48%)
  blocking collectives  76.2 us (23%)
  matrix products  48.8 us (15%)
  starting transfers between devices  15.6 us (5%)
  between operations  14 us (4%)
  other arithmetic  11 us (3%)
  local copies, waits for them, and re-layouts  5.29 us (2%)
    reduce_scatter x1, waiting for transfers between devices, local(): lax.psum_scatter(partial_grad, 'col', scatter_dimension=0, tiled=True)  84.9 us
    all_gather x1, waiting for transfers between devices, local(): up_piece = lax.all_gather(up_block, 'col', axis=0, tiled=True)  39.1 us
    all_to_all x1, blocking collectives, local(): got = lax.all_to_all(sent, 'row', split_axis=0, concat_axis=0, tiled=True)  25.1 us
    all_to_all x1, blocking collectives, row_gather(): got = lax.all_to_all(copies, 'row', split_axis=0, concat_axis=0, tiled=True)  23.5 us
    all_to_all x2, waiting for transfers between devices, row_gather(): got = lax.all_to_all(copies, 'row', split_axis=0, concat_axis=0, tiled=True)  23.1 us
    all_to_all x1, blocking collectives, local(): lax.all_to_all(packed, 'col', split_axis=1, concat_axis=0, tiled=True)  14.1 us
    all_to_all x1, blocking collectives, local(): lax.all_to_all(grad_out, 'col', split_axis=1, concat_axis=0, tiled=True)  13.4 us
    all_gather x1, waiting for transfers between devices, local(): gate_piece = lax.all_gather(gate_block, 'col', axis=0, tiled=True)  10.2 us
  transfers between devices with their start and end apart: 8, of which 6 were waited for; matrix products, arithmetic and copies ran while one was open for 16% of the time, Pallas kernels for 0%

commit v1 on v0

--- a/solution.py
+++ b/solution.py
@@ -36,7 +36,10 @@
     gain_tile = lax.dynamic_slice_in_dim(gain, lax.axis_index("col") * tile, tile)
     mine_rows = tokens.shape[0]
     lanes = 128
-    grid_grad = lax.all_to_all(grad_out, "col", split_axis=1, concat_axis=0, tiled=True)
+    grid_grad = jnp.concatenate(
+        lax.all_to_all(jnp.stack(jnp.split(grad_out, lax.axis_size("col"), axis=1)), "col", 0, 0),
+        axis=0,
+    )
     packed = jnp.concatenate(
         [
             tokens_wide.reshape(mine_rows, cols, tile),

time: 331 us -> 337 us (1.018)
  local copies, waits for them, and re-layouts: 5.29 us -> 16.8 us
  waiting for transfers between devices: 159 us -> 154 us
    unnamed x18 -> x35, local copies, waits for them, and re-layouts: 1.05 us -> 11.9 us
    reduce_scatter x1, waiting for transfers between devices: 84.9 us -> 79.3 us  [local(): lax.psum_scatter(partial_grad, 'col', scatter_dimension=0, tiled=True)]
  transfers between devices with their start and end apart: 8 -> 8, of which waited for: 6 -> 6; matrix products, arithmetic and copies ran while one was open for 16% -> 18% of each run, Pallas kernels for 0% -> 0%
where the time goes in v1:
time: 337 us; the launch traced here: 335 us
  waiting for transfers between devices  154 us (46%)
  blocking collectives  77.6 us (23%)
  matrix products  46.7 us (14%)
  local copies, waits for them, and re-layouts  16.8 us (5%)
  starting transfers between devices  15.3 us (5%)
  between operations  14 us (4%)
  other arithmetic  11 us (3%)
    reduce_scatter x1, waiting for transfers between devices, local(): lax.psum_scatter(partial_grad, 'col', scatter_dimension=0, tiled=True)  79.3 us
    all_gather x1, waiting for transfers between devices, local(): up_piece = lax.all_gather(up_block, 'col', axis=0, tiled=True)  38.9 us
    all_to_all x1, blocking collectives, local(): got = lax.all_to_all(sent, 'row', split_axis=0, concat_axis=0, tiled=True)  25.1 us
    all_to_all x1, blocking collectives, row_gather(): got = lax.all_to_all(copies, 'row', split_axis=0, concat_axis=0, tiled=True)  24.3 us
    all_to_all x2, waiting for transfers between devices, row_gather(): got = lax.all_to_all(copies, 'row', split_axis=0, concat_axis=0, tiled=True)  23.1 us
    all_to_all x1, blocking collectives, local(): lax.all_to_all(packed, 'col', split_axis=1, concat_axis=0, tiled=True)  14.3 us
    all_to_all x1, blocking collectives, local(): lax.all_to_all(jnp.stack(jnp.split(grad_out, lax.axis_size('col'), axis=1...  13.9 us
    unnamed x35, local copies, waits for them, and re-layouts  11.9 us
  transfers between devices with their start and end apart: 8, of which 6 were waited for; matrix products, arithmetic and copies ran while one was open for 18% of the time, Pallas kernels for 0%

profile of v1, /device:TPU:1, one launch (start us, length us, event | category | flops | bytes accessed | tf_op | source)
XLA Modules:
  0.0 335.3 jit_solution(6340046844845479934)
XLA Ops:
  7.2 1.4 fusion.4
  8.6 0.7 slice.76
  9.4 0.9 constant_dynamic-update-slice_fusion.15
  10.3 0.9 constant_dynamic-update-slice_fusion.14
  11.1 0.7 constant_dynamic-update-slice_fusion.13
  11.8 0.7 constant_dynamic-update-slice_fusion.12
  12.5 0.7 constant_dynamic-update-slice_fusion.11
  13.2 0.7 constant_dynamic-update-slice_fusion.10
  13.9 0.7 constant_dynamic-update-slice_fusion.9
  14.6 0.7 constant_dynamic-update-slice_fusion.8
  15.3 0.7 constant_dynamic-update-slice_fusion.7
  16.0 0.7 constant_dynamic-update-slice_fusion.6
  16.7 0.7 constant_dynamic-update-slice_fusion.5
  17.4 0.7 constant_dynamic-update-slice_fusion.4
  18.1 0.7 constant_dynamic-update-slice_fusion.3
  18.8 0.7 constant_dynamic-update-slice_fusion.2
  19.5 0.7 constant_dynamic-update-slice_fusion.1
  20.2 0.7 constant_dynamic-update-slice_fusion
  20.9 13.9 %all_to_all.45 = bf16[16,8,512]{2,1,0:T(8,128)(2,1)S(1)} all-to-all(bf16[16,8,512]{2,1,0:T(8,128)(2,1)S(1)} %constant_dynamic-update-slice_fusion), channel_id=1, replica_groups=mesh['row'=8,'col'=16] {'col'}, dimensions={0} | all-to-all | bytes 262144 | tf_op jit(solution)/shard_map/all_to_all | solution.py:40
  34.9 24.3 %all_to_all.46 = bf16[8,128,512]{2,1,0:T(8,128)(2,1)S(1)} all-to-all(bf16[8,128,512]{2,1,0:T(8,128)(2,1)S(1)} %broadcast_in_dim.15), channel_id=1, replica_groups=mesh['row'=8,'col'=16] {'row'}, dimensions={0} | all-to-all | bytes 2097152 | tf_op jit(solution)/shard_map/all_to_all | solution.py:25
  59.2 1.0 copy-done.4
  60.2 7.3 %fusion.13 = f32[1024,3584]{1,0:T(8,128)} fusion(bf16[1024,512]{1,0:T(8,128)(2,1)S(1)} %bitcast.71, bf16[3584,512]{1,0:T(8,128)(2,1)S(1)} %copy-done.8), kind=kOutput, calls=%fused_computation.54 | convolution fusion | flops 3758096384 | bytes 19398656 | tf_op jit(solution)/shard_map/td,fd->tf/dot_general | solution.py:58
  67.7 3.2 fusion.14
  70.9 79.3 %reduce-scatter.2.cloned.1.call-done = f32[64,3584]{1,0:T(8,128)} async-done(((f32[1024,3584]{1,0:T(8,128)}), f32[64,3584]{1,0:T(8,128)}) %reduce-scatter.2.cloned.1.call-update) | async-done | bytes 917520 | tf_op jit(solution)/shard_map/reduce_scatter | solution.py:62
  150.1 2.5 multiply_convert_fusion
  153.6 14.3 %all_to_all.47 = f32[8,16,640]{2,0,1:T(8,128)S(1)} all-to-all(f32[8,16,640]{2,0,1:T(8,128)S(1)} %pad_maximum_fusion.3), channel_id=1, replica_groups=mesh['row'=8,'col'=16] {'col'}, dimensions={1} | all-to-all | bytes 655360 | tf_op jit(solution)/shard_map/all_to_all | solution.py:50
  168.6 5.9 %all-to-all-start.4 = ((f32[8,1,128]{2,1,0:T(1,128)}), f32[8,1,128]{2,1,0:T(1,128)S(1)}, u32[]{:S(2)}, u32[]{:S(2)}) async-start(f32[8,1,128]{2,1,0:T(1,128)} %broadcast_in_dim.19), calls=%async_computation.5 | async-start | bytes 8192 | tf_op jit(solution)/shard_map/all_to_all | solution.py:25
  174.6 6.4 %all-to-all-done.4 = f32[8,1,128]{2,1,0:T(1,128)S(1)} async-done(((f32[8,1,128]{2,1,0:T(1,128)}), f32[8,1,128]{2,1,0:T(1,128)S(1)}, u32[]{:S(2)}, u32[]{:S(2)}) %all-to-all-start.4) | async-done | bytes 4128 | tf_op jit(solution)/shard_map/all_to_all | solution.py:25
  181.0 1.1 broadcast_in_dim.17
  182.1 3.6 %all-to-all-start.3 = ((bf16[8,128,512]{2,1,0:T(8,128)(2,1)}), bf16[8,128,512]{2,1,0:T(8,128)(2,1)S(1)}, u32[]{:S(2)}, u32[]{:S(2)}) async-start(bf16[8,128,512]{2,1,0:T(8,128)(2,1)} %broadcast_in_dim.17), calls=%async_computation.4 | async-start | bytes 2097152 | tf_op jit(solution)/shard_map/all_to_all | solution.py:25
  185.9 0.8 slice.77
  186.7 16.7 %all-to-all-done.3 = bf16[8,128,512]{2,1,0:T(8,128)(2,1)S(1)} async-done(((bf16[8,128,512]{2,1,0:T(8,128)(2,1)}), bf16[8,128,512]{2,1,0:T(8,128)(2,1)S(1)}, u32[]{:S(2)}, u32[]{:S(2)}) %all-to-all-start.3) | async-done | bytes 1048608 | tf_op jit(solution)/shard_map/all_to_all | solution.py:25
  203.4 1.3 fusion.2
  204.7 10.4 %all-gather.7.cloned.1.call-done = bf16[1024,3584]{1,0:T(8,128)(2,1)} async-done(((bf16[64,3584]{1,0:T(8,128)(2,1)}), bf16[1024,3584]{1,0:T(8,128)(2,1)}) %all-gather.7.cloned.1.call-update) | async-done | bytes 7340048 | tf_op jit(solution)/shard_map/all_gather | solution.py:70
  215.1 9.3 %fusion.16 = bf16[512,3584]{1,0:T(8,128)(2,1)} fusion(bf16[1024,512]{1,0:T(8,128)(2,1)} %fusion.2, bf16[1024,3584]{1,0:T(8,128)(2,1)} %all-gather.7.cloned.1.call-done), kind=kOutput, calls=%fused_computation.57 | convolution fusion | flops 3758096384 | bytes 12058624 | tf_op jit(solution)/shard_map/td,tf->df/dot_general | solution.py:72
  224.3 38.9 %all-gather.9.cloned.1.call-done = bf16[1024,3584]{1,0:T(8,128)(2,1)} async-done(((bf16[64,3584]{1,0:T(8,128)(2,1)}), bf16[1024,3584]{1,0:T(8,128)(2,1)}) %all-gather.9.cloned.1.call-update) | async-done | bytes 7340048 | tf_op jit(solution)/shard_map/all_gather | solution.py:71
  263.3 7.5 %fusion.15 = f32[1024,512]{1,0:T(8,128)S(1)} fusion(bf16[1024,3584]{1,0:T(8,128)(2,1)} %all-gather.7.cloned.1.call-done, bf16[512,3584]{1,0:T(8,128)(2,1)} %param.17), kind=kOutput, calls=%fused_computation.56 | convolution fusion | flops 3758096384 | bytes 13107200 | tf_op jit(solution)/shard_map/tf,df->td/dot_general | solution.py:76
  270.8 5.1 %fusion.12 = (bf16[1024,512]{1,0:T(8,128)(2,1)}, f32[512]{0:T(512)S(1)}) fusion(f32[1024]{0:T(1024)S(1)} %bitcast.80, bf16[8,128,512]{2,1,0:T(8,128)(2,1)S(1)} %all-to-all-done.3, f32[1024,512]{1,0:T(8,128)S(1)} %fusion.15, bf16[1024,3584]{1,0:T(8,128)(2,1)S(1)} %copy-done.7, bf16[512,3584]{1,0:T(8,128)(2,1)S(1)} %copy-done.9), kind=kOutput, calls=%fused_computation.53 | convolution fusion | flops 3761241600 | bytes 15210496 | tf_op jit(solution)/shard_map/tf,df->td/dot_general | solution.py:77
  276.0 1.4 pad_maximum_fusion.1
  277.4 25.1 %all_to_all.48 = bf16[8,136,512]{2,1,0:T(8,128)(2,1)S(1)} all-to-all(bf16[8,136,512]{2,1,0:T(8,128)(2,1)S(1)} %pad_maximum_fusion.1), channel_id=1, replica_groups=mesh['row'=8,'col'=16] {'row'}, dimensions={0} | all-to-all | bytes 2228224 | tf_op jit(solution)/shard_map/all_to_all | solution.py:88
  302.8 0.9 pad_maximum_fusion.2
  303.6 5.4 %all-to-all-start.6 = ((f32[16,9,512]{2,1,0:T(8,128)}), f32[16,9,512]{2,1,0:T(8,128)S(1)}, u32[]{:S(2)}, u32[]{:S(2)}) async-start(f32[16,9,512]{2,1,0:T(8,128)} %pad_maximum_fusion.2), calls=%async_computation.7 | async-start | bytes 1048576 | tf_op jit(solution)/shard_map/all_to_all | solution.py:97
  309.0 8.7 %convolution_convert_fusion = bf16[512,3584]{1,0:T(8,128)(2,1)} fusion(bf16[1024,512]{1,0:T(8,128)(2,1)S(1)} %copy-done.3, bf16[1024,3584]{1,0:T(8,128)(2,1)} %all-gather.9.cloned.1.call-done), kind=kOutput, calls=%fused_computation | convolution fusion | flops 3759931392 | bytes 12058624 | tf_op jit(solution)/shard_map/td,tf->df/dot_general | solution.py:100
  317.7 1.6 all-to-all-done.6
  319.3 0.6 slice.84
  320.2 0.8 add_convert_fusion
  321.0 5.7 %convolution_convert_fusion.1 = bf16[2560,512]{1,0:T(8,128)(2,1)S(1)} fusion(bf16[1024,2560]{1,0:T(8,128)(2,1)} %all-gather.11.cloned.1.call-done, bf16[1024,512]{1,0:T(8,128)(2,1)} %bitcast.73), kind=kOutput, calls=%fused_computation.1 | convolution fusion | flops 2685665280 | bytes 8912896 | tf_op jit(solution)/shard_map/tf,td->fd/dot_general | solution.py:101
  326.7 2.1 pad_maximum_fusion
  (53 shorter events, 2.8 us)
Async XLA Ops:
  7.2 60.4 %all-gather.5.cloned.1.call-start = ((), (), s32[]{:S(2)}) async-start(), calls=%async_computation.8 | async-start | bytes 2228224 | tf_op jit(solution)/shard_map/all_gather | solution.py:57
  9.3 140.8 %reduce-scatter.2.cloned.1.call-start = ((), (), s32[]{:S(2)}) async-start(), calls=%async_computation.9 | async-start | bytes 15597568 | tf_op jit(solution)/shard_map/reduce_scatter | solution.py:62
  9.4 50.9 %copy-start.8 = (bf16[3584,512]{1,0:T(8,128)(2,1)S(1)}, bf16[3584,512]{1,0:T(8,128)(2,1)}, u32[]{:S(2)}) copy-start(bf16[3584,512]{1,0:T(8,128)(2,1)} %param.19) | copy-start | bytes 11010052
  59.2 1.0 copy-start.4
  67.6 82.6 %copy-start.1 = (bf16[64,3584]{1,0:T(8,128)(2,1)S(1)}, bf16[64,3584]{1,0:T(8,128)(2,1)}, u32[]{:S(2)}) copy-start(bf16[64,3584]{1,0:T(8,128)(2,1)} %param.16) | copy-start | bytes 1376260
  67.6 82.5 %copy-start.2 = (bf16[64,3584]{1,0:T(8,128)(2,1)S(1)}, bf16[64,3584]{1,0:T(8,128)(2,1)}, u32[]{:S(2)}) copy-start(bf16[64,3584]{1,0:T(8,128)(2,1)} %param.15) | copy-start | bytes 1376260
  67.6 147.5 %all-gather.7.cloned.1.call-start = ((), (), s32[]{:S(2)}) async-start(), calls=%async_computation.10 | async-start | bytes 7798784 | tf_op jit(solution)/shard_map/all_gather | solution.py:70
  70.9 82.4 %copy-start = (bf16[8,8192]{1,0:T(8,128)(2,1)S(1)}, bf16[8,8192]{1,0:T(8,128)(2,1)}, u32[]{:S(2)}) copy-start(bf16[8,8192]{1,0:T(8,128)(2,1)} %param.12) | copy-start | bytes 393220
  152.7 34.0 %copy-start.6 = (f32[8192]{0:T(1024)S(1)}, f32[8192]{0:T(1024)}, u32[]{:S(2)}) copy-start(f32[8192]{0:T(1024)} %param.13) | copy-start | bytes 98308
  152.7 110.5 %all-gather.9.cloned.1.call-start = ((), (), s32[]{:S(2)}) async-start(), calls=%async_computation.11 | async-start | bytes 7798784 | tf_op jit(solution)/shard_map/all_gather | solution.py:71
  168.6 12.4 %all-to-all-start.4 = ((f32[8,1,128]{2,1,0:T(1,128)}), f32[8,1,128]{2,1,0:T(1,128)S(1)}, u32[]{:S(2)}, u32[]{:S(2)}) async-start(f32[8,1,128]{2,1,0:T(1,128)} %broadcast_in_dim.19), calls=%async_computation.5 | async-start | bytes 8192 | tf_op jit(solution)/shard_map/all_to_all | solution.py:25
  182.1 21.3 %all-to-all-start.3 = ((bf16[8,128,512]{2,1,0:T(8,128)(2,1)}), bf16[8,128,512]{2,1,0:T(8,128)(2,1)S(1)}, u32[]{:S(2)}, u32[]{:S(2)}) async-start(bf16[8,128,512]{2,1,0:T(8,128)(2,1)} %broadcast_in_dim.17), calls=%async_computation.4 | async-start | bytes 2097152 | tf_op jit(solution)/shard_map/all_to_all | solution.py:25
  185.7 135.3 %all-gather.11.cloned.1.call-start = ((), (), s32[]{:S(2)}) async-start(), calls=%async_computation.12 | async-start | bytes 5570560 | tf_op jit(solution)/shard_map/all_gather | solution.py:75
  263.2 7.5 %copy-start.7 = (bf16[1024,3584]{1,0:T(8,128)(2,1)S(1)}, bf16[1024,3584]{1,0:T(8,128)(2,1)}, u32[]{:S(2)}) copy-start(bf16[1024,3584]{1,0:T(8,128)(2,1)} %all-gather.9.cloned.1.call-done) | copy-start | bytes 22020100
  263.3 7.5 %copy-start.9 = (bf16[512,3584]{1,0:T(8,128)(2,1)S(1)}, bf16[512,3584]{1,0:T(8,128)(2,1)}, u32[]{:S(2)}) copy-start(bf16[512,3584]{1,0:T(8,128)(2,1)} %param.18) | copy-start | bytes 11010052
  276.0 33.0 %copy-start.3 = (bf16[1024,512]{1,0:T(8,128)(2,1)S(1)}, bf16[1024,512]{1,0:T(8,128)(2,1)}, u32[]{:S(2)}) copy-start(bf16[1024,512]{1,0:T(8,128)(2,1)} %fusion.2) | copy-start | bytes 3145732
  303.6 15.6 %all-to-all-start.6 = ((f32[16,9,512]{2,1,0:T(8,128)}), f32[16,9,512]{2,1,0:T(8,128)S(1)}, u32[]{:S(2)}, u32[]{:S(2)}) async-start(f32[16,9,512]{2,1,0:T(8,128)} %pad_maximum_fusion.2), calls=%async_computation.7 | async-start | bytes 1048576 | tf_op jit(solution)/shard_map/all_to_all | solution.py:97
  309.0 11.2 %copy-start.5 = (bf16[8,8192]{1,0:T(8,128)(2,1)S(1)}, bf16[8,8192]{1,0:T(8,128)(2,1)}, u32[]{:S(2)}) copy-start(bf16[8,8192]{1,0:T(8,128)(2,1)} %param.14) | copy-start | bytes 393220
Sparse Core Ops, SparseCore 0:
  10.2 40.1 all-gather.4
  67.7 82.3 reduce-scatter.1
  152.8 62.2 all-gather.6
  216.6 46.5 all-gather.8
  264.8 56.1 all-gather.10
